TPU v7x, 256 devices: a whole 4x4x8 slice. The times are simulated.
256 devices in a mesh: fsdp: 8 (over z_lo, core), seq: 32 (over x, z_hi, y).
Axes of the slice: x: 4, y: 4, z: 8 (z_hi: 2, z_lo: 4; z = z_hi * 4 + z_lo), core: 2. Of those that a mesh axis runs over, the one named last changes fastest.
Arguments:
- tokens: bfloat16 [2, 4096, 4096], P(None, 'seq'), may hold values from -6 to 6
- positions: int32 [2, 4096], replicated, may hold values from 0 to 4095, as said below
- cached_len: int32 [2], replicated, may hold values from 16 to 4096, as said below
- cache_keys: bfloat16 [2, 4096, 8, 128], P(None, 'seq', 'fsdp'), may hold values from -6 to 6
- cache_values: bfloat16 [2, 4096, 8, 128], P(None, 'seq', 'fsdp'), may hold values from -6 to 6
- w_query: bfloat16 [4096, 4096], P('seq', 'fsdp')
- w_key: bfloat16 [4096, 1024], P('seq', 'fsdp')
- w_value: bfloat16 [4096, 1024], P('seq', 'fsdp'), may hold values from -0.09375 to 0.09375
- w_out_t: bfloat16 [4096, 4096], P('seq', 'fsdp'), may hold values from -1.5 to 1.5
Outputs:
- mixed: bfloat16 [2, 4096, 4096], P(None, 'seq', 'fsdp')
- new_keys: bfloat16 [2, 4096, 8, 128], P(None, 'seq', 'fsdp')
- new_values: bfloat16 [2, 4096, 8, 128], P(None, 'seq', 'fsdp')
Inputs may be any that keep to these rules, and one draw needn't show every extreme that they name: For each request the stored order is a permutation of 0 to 4095: the span is cut into 64 blocks of 64 positions, and the 128 stored rows of each index of seq are one block b followed by the block 63 - b, each in rising order; b is drawn per request and index. `cached_len`: some request has exactly 4096 cached positions.
All inputs are finite; a program needn't handle non-finite values.
Results may differ from a plain program's by a relative error of at most 0.015.
The roundings to bfloat16 on the way count: a program that leaves them out, or rounds other values in their place, can miss the bound.
Values may be sent and summed in bfloat16 or wider, within the bound.
No kernel may reach another device: no remote copies, remote signals or barrier semaphores. Data moves between devices by JAX's collectives and lax.ppermute only.
A program may use at most 128 MiB of HBM per device.

v0:
```python
import math
import jax
import jax.numpy as jnp
from jax import lax
from jax.sharding import PartitionSpec as P

SINKS = 4
NEGATIVE = -1e30


def attend_block(running_state, queries, key_block, value_block, allowed):
    top_old, denom_old, numer_old = running_state
    scores = jnp.einsum("rqkgd,rpkd->rkgqp", queries, key_block, preferred_element_type=jnp.float32)
    scores = scores * (1.0 / math.sqrt(queries.shape[-1]))
    visible = allowed[:, None, None, :, :]
    scores = jnp.where(visible, scores, NEGATIVE)
    top_new = jnp.maximum(top_old, jnp.max(scores, axis=-1))
    rescale = jnp.exp(top_old - top_new)
    weights = jnp.where(visible, jnp.exp(scores - top_new[..., None]), 0.0)
    denom_new = denom_old * rescale + jnp.sum(weights, axis=-1)
    numer_new = numer_old * rescale[..., None] + jnp.einsum(
        "rkgqp,rpkd->rkgqd",
        weights.astype(jnp.bfloat16),
        value_block,
        preferred_element_type=jnp.float32,
    )
    return (top_new, denom_new, numer_new)


def shards(
    tokens, positions, cached_len, cache_keys, cache_values, w_query, w_key, w_value, w_out_t
):
    requests, rows, width = tokens.shape
    head_size = cache_keys.shape[3]
    kv_local = cache_keys.shape[2]
    group_size = w_query.shape[1] // (kv_local * head_size)
    seq_index = lax.axis_index("seq")
    seq_count = lax.axis_size("seq")
    window_len = rows * seq_count // 2
    my_positions = lax.dynamic_slice_in_dim(positions, seq_index * rows, rows, 1)
    flat_tokens = tokens.reshape(requests * rows, width)
    weight_pieces = (
        lax.all_gather(w_query, "seq", axis=0, tiled=True),
        lax.all_gather(w_key, "seq", axis=0, tiled=True),
        lax.all_gather(w_value, "seq", axis=0, tiled=True),
    )
    query_sum, key_sum, value_sum = tuple(
        (
            jnp.dot(flat_tokens, weight_piece, preferred_element_type=jnp.float32)
            for weight_piece in weight_pieces
        )
    )
    queries = query_sum.astype(jnp.bfloat16).reshape(
        requests, rows, kv_local, group_size, head_size
    )
    new_keys = key_sum.astype(jnp.bfloat16).reshape(requests, rows, kv_local, head_size)
    new_values = value_sum.astype(jnp.bfloat16).reshape(requests, rows, kv_local, head_size)
    lengths = cached_len[:, None]
    window_floor = lengths + my_positions - window_len
    running_state = (
        jnp.full((requests, kv_local, group_size, rows), NEGATIVE, jnp.float32),
        jnp.zeros((requests, kv_local, group_size, rows), jnp.float32),
        jnp.zeros((requests, kv_local, group_size, rows, head_size), jnp.float32),
    )
    block_pieces = (
        lax.all_gather(cache_keys, "seq", axis=1, tiled=True),
        lax.all_gather(cache_values, "seq", axis=1, tiled=True),
    )
    key_pos = jnp.arange(block_pieces[0].shape[1], dtype=jnp.int32)
    key_pos = key_pos[None, None, :]
    allowed = (key_pos < lengths[:, :, None]) & (
        (key_pos < SINKS) | (key_pos > window_floor[:, :, None])
    )
    running_state = attend_block(running_state, queries, block_pieces[0], block_pieces[1], allowed)
    block_pieces = (
        lax.all_gather(new_keys, "seq", axis=1, tiled=True),
        lax.all_gather(new_values, "seq", axis=1, tiled=True),
    )
    before = my_positions[:, :, None] - positions[:, None, :]
    allowed = (before >= 0) & (before < window_len)
    running_state = attend_block(running_state, queries, block_pieces[0], block_pieces[1], allowed)
    top_final, denom_final, numer_final = running_state
    attended = (numer_final / denom_final[..., None]).astype(jnp.bfloat16)
    attended = jnp.transpose(attended, (0, 3, 1, 2, 4)).reshape(
        requests * rows, kv_local * group_size * head_size
    )
    partial_out = lax.dot_general(
        attended,
        lax.all_gather(w_out_t, "seq", axis=0, tiled=True),
        (((1,), (1,)), ((), ())),
        preferred_element_type=jnp.float32,
    )
    mixed = lax.psum_scatter(
        partial_out.reshape(requests, rows, width).astype(jnp.bfloat16),
        "fsdp",
        scatter_dimension=2,
        tiled=True,
    )
    return (mixed, new_keys, new_values)


def solution(mesh):
    placed = (
        P(None, "seq", None),
        P(),
        P(),
        P(None, "seq", "fsdp", None),
        P(None, "seq", "fsdp", None),
        P("seq", "fsdp"),
        P("seq", "fsdp"),
        P("seq", "fsdp"),
        P("seq", "fsdp"),
    )
    return jax.shard_map(
        shards,
        mesh=mesh,
        in_specs=placed,
        out_specs=(
            P(None, "seq", "fsdp"),
            P(None, "seq", "fsdp", None),
            P(None, "seq", "fsdp", None),
        ),
        check_vma=False,
    )
```

profile of v0, /device:TPU:6, one launch (start us, length us, event | category | flops | bytes accessed | tf_op | source)
XLA Modules:
  0.0 814.5 jit_solution(16966259465033407726)
XLA Ops:
  7.2 0.7 all-gather.15.cloned.1.call-update
  8.0 0.7 all-gather.19.cloned.1.call-update
  8.7 0.7 all-gather.9.cloned.1.call-update
  9.4 84.8 %all-gather.15.cloned.1.call-done = bf16[4096,128]{1,0:T(8,128)(2,1)} async-done(((bf16[128,128]{1,0:T(8,128)(2,1)}), bf16[4096,128]{1,0:T(8,128)(2,1)}) %all-gather.15.cloned.1.call-update) | async-done | bytes 1048592 | tf_op jit(solution)/shard_map/all_gather | solution.py:44
  94.2 2.6 convolution_convert_fusion.3
  96.8 0.0 all-gather.11.cloned.1.call-start
  96.8 0.5 all-gather.11.cloned.1.call-update
  97.4 1.6 copy.14
  99.0 0.0 all-gather.21.cloned.1.call-start
  99.1 74.3 %all-gather.19.cloned.1.call-done = bf16[4096,128]{1,0:T(8,128)(2,1)} async-done(((bf16[128,128]{1,0:T(8,128)(2,1)}), bf16[4096,128]{1,0:T(8,128)(2,1)}) %all-gather.19.cloned.1.call-update) | async-done | bytes 1048592 | tf_op jit(solution)/shard_map/all_gather | solution.py:45
  173.3 1.9 convolution_convert_fusion.2
  175.3 0.7 copy.17
  176.1 0.7 all-gather.23.cloned.1.call-update
  176.9 0.7 iota_compare_fusion.1
  177.6 0.8 add_add_fusion
  178.4 3.5 fusion.16
  181.9 100.4 %all-gather.9.cloned.1.call-done = bf16[4096,512]{1,0:T(8,128)(2,1)} async-done(((bf16[128,512]{1,0:T(8,128)(2,1)}), bf16[4096,512]{1,0:T(8,128)(2,1)}) %all-gather.9.cloned.1.call-update) | async-done | bytes 4194320 | tf_op jit(solution)/shard_map/all_gather | solution.py:43
  282.3 4.1 convolution_convert_fusion.1
  286.4 1.0 reshape.173
  287.4 84.5 %all-gather.17.cloned.1.call-done = bf16[2,4096,1,128]{3,1,0,2:T(8,128)(2,1)} async-done(((bf16[2,128,1,128]{3,1,0,2:T(8,128)(2,1)}), bf16[2,4096,1,128]{3,1,0,2:T(8,128)(2,1)}) %all-gather.17.cloned.1.call-update) | async-done | bytes 2097168 | tf_op jit(solution)/shard_map/all_gather | solution.py:76
  371.9 9.3 %fusion.1 = (f32[2,4,128]{2,1,0:T(4,128)S(1)}, f32[2,4096,128,4]{1,2,3,0:T(8,128)}) fusion(pred[2,128,4096]{2,1,0:T(8,128)(4,1)S(1)} %get-tuple-element.18, bf16[2,128,4,128]{3,2,1,0:T(4,128)(2,1)S(1)} %reshape.173, bf16[2,4096,1,128]{3,1,0,2:T(8,128)(2,1)} %all-gather.17.cloned.1.call-done), kind=kOutput, calls=%fused_computation.5 | convolution fusion | flops 1086323712 | bytes 20189184 | tf_op jit(solution)/shard_map/rqkgd,rpkd->rkgqp/dot_general | solution.py:13
  381.2 79.6 %all-gather.11.cloned.1.call-done = bf16[2,4096,1,128]{3,1,0,2:T(8,128)(2,1)} async-done(((bf16[2,128,1,128]{3,1,0,2:T(8,128)(2,1)}), bf16[2,4096,1,128]{3,1,0,2:T(8,128)(2,1)}) %all-gather.11.cloned.1.call-update) | async-done | bytes 2097168 | tf_op jit(solution)/shard_map/all_gather | solution.py:66
  460.8 10.4 %fusion = (f32[2,4,128]{2,1,0:T(4,128)S(1)}, f32[2,128,4,4096]{3,1,2,0:T(8,128)}) fusion(pred[2,128,4096]{2,1,0:T(8,128)(4,1)} %get-tuple-element.17, bf16[2,4096,1,128]{3,1,0,2:T(8,128)(2,1)} %all-gather.11.cloned.1.call-done, bf16[2,128,4,128]{3,2,1,0:T(4,128)(2,1)S(1)} %reshape.173), kind=kOutput, calls=%fused_computation.4 | convolution fusion | flops 1086323712 | bytes 20189184 | tf_op jit(solution)/shard_map/rqkgd,rpkd->rkgqp/dot_general | solution.py:13
  471.2 8.7 %fusion.2 = f32[2,4,128]{2,1,0:T(4,128)S(1)} fusion(f32[2,128,4,4096]{3,1,2,0:T(8,128)} %get-tuple-element.14, f32[2,4,128]{2,1,0:T(4,128)S(1)} %get-tuple-element.12, pred[2,128,4096]{2,1,0:T(8,128)(4,1)S(1)} %copy-done.1), kind=kLoop, calls=%fused_computation.6 | loop fusion | flops 20970496 | bytes 17833984 | tf_op jit(solution)/shard_map/reduce_sum | solution.py:20
  479.9 5.0 fusion.4
  484.9 72.1 %all-gather.13.cloned.1.call-done = bf16[2,4096,1,128]{1,3,0,2:T(8,128)(2,1)} async-done(((bf16[2,128,1,128]{1,3,0,2:T(8,128)(2,1)}), bf16[2,4096,1,128]{1,3,0,2:T(8,128)(2,1)}) %all-gather.13.cloned.1.call-update) | async-done | bytes 2097168 | tf_op jit(solution)/shard_map/all_gather | solution.py:67
  557.0 10.6 %fusion.34 = f32[2,4,128,128]{2,3,1,0:T(8,128)} fusion(bf16[2,4096,1,128]{1,3,0,2:T(8,128)(2,1)} %all-gather.13.cloned.1.call-done, f32[2,128,4,4096]{3,1,2,0:T(8,128)} %get-tuple-element.14, f32[2,4,128]{2,1,0:T(4,128)S(1)} %get-tuple-element.12, pred[2,128,4096]{2,1,0:T(8,128)(4,1)} %get-tuple-element.17, f32[2,4,128]{2,1,0:T(4,128)S(1)} %get-tuple-element.7, ...), kind=kOutput, calls=%fused_computation.32 | convolution fusion | flops 1094975488 | bytes 20459520 | tf_op jit(solution)/shard_map/rkgqp,rpkd->rkgqd/dot_general | solution.py:21
  567.7 87.5 %all-gather.21.cloned.1.call-done = bf16[2,4096,1,128]{1,3,0,2:T(8,128)(2,1)} async-done(((bf16[2,128,1,128]{1,3,0,2:T(8,128)(2,1)}), bf16[2,4096,1,128]{1,3,0,2:T(8,128)(2,1)}) %all-gather.21.cloned.1.call-update) | async-done | bytes 2097168 | tf_op jit(solution)/shard_map/all_gather | solution.py:77
  655.1 9.7 %fusion.44 = bf16[2,4,128,128]{2,3,1,0:T(8,128)(2,1)S(1)} fusion(f32[2,4,128,128]{2,3,1,0:T(8,128)} %fusion.34, bf16[2,4096,1,128]{1,3,0,2:T(8,128)(2,1)} %all-gather.21.cloned.1.call-done, f32[2,4096,128,4]{1,2,3,0:T(8,128)} %get-tuple-element.16, f32[2,4,128]{2,1,0:T(4,128)S(1)} %get-tuple-element.11, pred[2,128,4096]{2,1,0:T(8,128)(4,1)S(1)} %get-tuple-element.18, ...), kind=kOutput, calls=%fused_computation.37 | convolution fusion | flops 1095106560 | bytes 20717568 | tf_op jit(solution)/shard_map/rkgqp,rpkd->rkgqd/dot_general | solution.py:21
  664.9 100.7 %all-gather.23.cloned.1.call-done = bf16[4096,512]{1,0:T(8,128)(2,1)} async-done(((bf16[128,512]{1,0:T(8,128)(2,1)}), bf16[4096,512]{1,0:T(8,128)(2,1)}) %all-gather.23.cloned.1.call-update) | async-done | bytes 4194320 | tf_op jit(solution)/shard_map/all_gather | solution.py:89
  765.6 4.8 convolution_convert_fusion
  770.5 37.5 %reduce-scatter.2.cloned.1.call-done = bf16[2,128,512]{2,1,0:T(8,128)(2,1)} async-done(((bf16[2,128,4096]{2,1,0:T(8,128)(2,1)}), bf16[2,128,512]{2,1,0:T(8,128)(2,1)}) %reduce-scatter.2.cloned.1.call-update) | async-done | bytes 262160 | tf_op jit(solution)/shard_map/reduce_scatter | solution.py:93
  (29 shorter events, 0.4 us)
Async XLA Ops:
  7.2 87.0 %copy-start = (bf16[2,128,4096]{2,1,0:T(8,128)(2,1)S(1)}, bf16[2,128,4096]{2,1,0:T(8,128)(2,1)}, u32[]{:S(2)}) copy-start(bf16[2,128,4096]{2,1,0:T(8,128)(2,1)} %param.9) | copy-start | bytes 6291460
  7.2 87.0 %all-gather.15.cloned.1.call-start = ((), (), s32[]{:S(2)}) async-start(), calls=%async_computation.4 | async-start | bytes 1081344 | tf_op jit(solution)/shard_map/all_gather | solution.py:44
  7.9 165.4 %all-gather.19.cloned.1.call-start = ((), (), s32[]{:S(2)}) async-start(), calls=%async_computation.6 | async-start | bytes 1081344 | tf_op jit(solution)/shard_map/all_gather | solution.py:45
  8.7 273.6 %all-gather.9.cloned.1.call-start = ((), (), s32[]{:S(2)}) async-start(), calls=%async_computation.1 | async-start | bytes 4325376 | tf_op jit(solution)/shard_map/all_gather | solution.py:43
  9.4 362.5 %all-gather.17.cloned.1.call-start = ((), (), s32[]{:S(2)}) async-start(), calls=%async_computation.5 | async-start | bytes 2162688 | tf_op jit(solution)/shard_map/all_gather | solution.py:76
  96.8 364.0 %all-gather.11.cloned.1.call-start = ((), (), s32[]{:S(2)}) async-start(), calls=%async_computation.2 | async-start | bytes 2162688 | tf_op jit(solution)/shard_map/all_gather | solution.py:66
  97.4 459.7 %all-gather.13.cloned.1.call-start = ((), (), s32[]{:S(2)}) async-start(), calls=%async_computation.3 | async-start | bytes 2162688 | tf_op jit(solution)/shard_map/all_gather | solution.py:67
  99.0 556.1 %all-gather.21.cloned.1.call-start = ((), (), s32[]{:S(2)}) async-start(), calls=%async_computation.7 | async-start | bytes 2162688 | tf_op jit(solution)/shard_map/all_gather | solution.py:77
  175.3 205.9 %copy-start.2 = (bf16[256,128]{1,0:T(8,128)(2,1)}, bf16[256,128]{1,0:T(8,128)(2,1)S(1)}, u32[]{:S(2)}) copy-start(bf16[256,128]{1,0:T(8,128)(2,1)S(1)} %convolution_convert_fusion.2) | copy-start | bytes 196612
  176.0 589.6 %all-gather.23.cloned.1.call-start = ((), (), s32[]{:S(2)}) async-start(), calls=%async_computation.8 | async-start | bytes 4325376 | tf_op jit(solution)/shard_map/all_gather | solution.py:89
  176.8 631.2 %reduce-scatter.2.cloned.1.call-start = ((), (), s32[]{:S(2)}) async-start(), calls=%async_computation.9 | async-start | bytes 2359296 | tf_op jit(solution)/shard_map/reduce_scatter | solution.py:93
  460.8 10.4 %copy-start.1 = (pred[2,128,4096]{2,1,0:T(8,128)(4,1)S(1)}, pred[2,128,4096]{2,1,0:T(8,128)(4,1)}, u32[]{:S(2)}) copy-start(pred[2,128,4096]{2,1,0:T(8,128)(4,1)} %get-tuple-element.17) | copy-start | bytes 3145732
  460.8 19.1 %slice-start = ((s8[16777216]{0:T(1024)(128)(4,1)}), s8[4194304]{0:T(1024)(128)(4,1)S(1)}, s32[]{:S(2)}) async-start(s8[16777216]{0:T(1024)(128)(4,1)} %bitcast.122), calls=%async_computation.10 | async-start | bytes 8388608
  460.8 19.1 %slice-start.1 = ((s8[16777216]{0:T(1024)(128)(4,1)}), s8[4194304]{0:T(1024)(128)(4,1)S(1)}, s32[]{:S(2)}) async-start(s8[16777216]{0:T(1024)(128)(4,1)} %bitcast.122), calls=%async_computation.11 | async-start | bytes 8388608
  460.8 19.1 %slice-start.2 = ((s8[16777216]{0:T(1024)(128)(4,1)}), s8[4194304]{0:T(1024)(128)(4,1)S(1)}, s32[]{:S(2)}) async-start(s8[16777216]{0:T(1024)(128)(4,1)} %bitcast.122), calls=%async_computation.12 | async-start | bytes 8388608
  471.2 8.7 %slice-start.3 = ((s8[16777216]{0:T(1024)(128)(4,1)}), s8[4194304]{0:T(1024)(128)(4,1)S(1)}, s32[]{:S(2)}) async-start(s8[16777216]{0:T(1024)(128)(4,1)} %bitcast.122), calls=%async_computation.13 | async-start | bytes 8388608
Sparse Core Ops, SparseCore 0:
  11.4 82.7 all-gather.14
  97.6 75.6 all-gather.18
  176.9 105.3 all-gather.8
  286.3 85.6 all-gather.16
  375.3 85.4 all-gather.10
  463.9 93.1 all-gather.12
  560.2 94.8 all-gather.20
  658.7 106.9 all-gather.22
  770.6 37.3 reduce-scatter.1
where the time goes:
time: 815 us; the launch traced here: 814 us
  waiting for transfers between devices  725 us (89%)
  matrix products  53.4 us (7%)
  other arithmetic  18.7 us (2%)
  between operations  14 us (2%)
    all_gather x1, waiting for transfers between devices, shards(): lax.all_gather(w_out_t, 'seq', axis=0, tiled=True)  101 us
    all_gather x1, waiting for transfers between devices, shards(): lax.all_gather(w_query, 'seq', axis=0, tiled=True)  100 us
    all_gather x1, waiting for transfers between devices, shards(): lax.all_gather(new_values, 'seq', axis=1, tiled=True)  87.5 us
    all_gather x1, waiting for transfers between devices, shards(): lax.all_gather(w_key, 'seq', axis=0, tiled=True)  84.8 us
    all_gather x1, waiting for transfers between devices, shards(): lax.all_gather(new_keys, 'seq', axis=1, tiled=True)  84.5 us
    all_gather x1, waiting for transfers between devices, shards(): lax.all_gather(cache_keys, 'seq', axis=1, tiled=True)  79.6 us
    all_gather x1, waiting for transfers between devices, shards(): lax.all_gather(w_value, 'seq', axis=0, tiled=True)  74.3 us
    all_gather x1, waiting for transfers between devices, shards(): lax.all_gather(cache_values, 'seq', axis=1, tiled=True)  72.1 us
  transfers between devices with their start and end apart: 9, of which 9 were waited for; matrix products, arithmetic and copies ran while one was open for 9% of the time, Pallas kernels for 0%

commit v1 on v0

--- a/solution.py
+++ b/solution.py
@@ -63,7 +63,9 @@
         jnp.zeros((requests, kv_local, group_size, rows, head_size), jnp.float32),
     )
     block_pieces = (
-        lax.all_gather(cache_keys, "seq", axis=1, tiled=True),
+        jnp.concatenate(
+            lax.all_to_all(jnp.stack([cache_keys] * lax.axis_size("seq")), "seq", 0, 0), axis=1
+        ),
         lax.all_gather(cache_values, "seq", axis=1, tiled=True),
     )
     key_pos = jnp.arange(block_pieces[0].shape[1], dtype=jnp.int32)

time: 815 us -> 755 us (0.926)
  waiting for transfers between devices: 725 us -> 653 us
    all_gather x1 -> x0, waiting for transfers between devices: 79.6 us -> none  [shards(): lax.all_gather(cache_keys, 'seq', axis=1, tiled=True)]
    all_to_all x0 -> x1, waiting for transfers between devices: none -> 43.5 us  [shards(): lax.all_to_all(jnp.stack([cache_keys] * lax.axis_size('seq')), 'seq', 0, 0)]
    all_gather x1, waiting for transfers between devices: 100 us -> 74.8 us  [shards(): lax.all_gather(w_query, 'seq', axis=0, tiled=True)]
    all_gather x1, waiting for transfers between devices: 84.5 us -> 74.8 us  [shards(): lax.all_gather(new_keys, 'seq', axis=1, tiled=True)]
  transfers between devices with their start and end apart: 9 -> 9, of which waited for: 9 -> 9; matrix products, arithmetic and copies ran while one was open for 9% -> 10% of each run, Pallas kernels for 0% -> 0%
where the time goes in v1:
time: 755 us
  waiting for transfers between devices  653 us (86%)
  matrix products  48.3 us (6%)
  other arithmetic  22.1 us (3%)
  between operations  14.3 us (2%)
  local copies, waits for them, and re-layouts  9.2 us (1%)
    all_gather x1, waiting for transfers between devices, shards(): lax.all_gather(w_out_t, 'seq', axis=0, tiled=True)  101 us
    all_gather x1, waiting for transfers between devices, shards(): lax.all_gather(new_values, 'seq', axis=1, tiled=True)  87.3 us
    all_gather x1, waiting for transfers between devices, shards(): lax.all_gather(w_key, 'seq', axis=0, tiled=True)  84.8 us
    all_gather x1, waiting for transfers between devices, shards(): lax.all_gather(w_value, 'seq', axis=0, tiled=True)  74.9 us
    all_gather x1, waiting for transfers between devices, shards(): lax.all_gather(new_keys, 'seq', axis=1, tiled=True)  74.8 us
    all_gather x1, waiting for transfers between devices, shards(): lax.all_gather(w_query, 'seq', axis=0, tiled=True)  74.8 us
    all_gather x1, waiting for transfers between devices, shards(): lax.all_gather(cache_values, 'seq', axis=1, tiled=True)  72.1 us
    all_to_all x1, waiting for transfers between devices, shards(): lax.all_to_all(jnp.stack([cache_keys] * lax.axis_size('seq')), 'seq', 0, 0)  43.5 us
  transfers between devices with their start and end apart: 9, of which 9 were waited for; matrix products, arithmetic and copies ran while one was open for 10% of the time, Pallas kernels for 0%

profile of v1, /device:TPU:6, one launch (start us, length us, event | category | flops | bytes accessed | tf_op | source)
XLA Modules:
  0.0 754.6 jit_solution(6176864919821950070)
XLA Ops:
  7.2 0.7 all-gather.12.cloned.1.call-update
  8.0 0.7 all-gather.16.cloned.1.call-update
  8.7 0.7 all-gather.8.cloned.1.call-update
  9.5 84.8 %all-gather.12.cloned.1.call-done = bf16[4096,128]{1,0:T(8,128)(2,1)} async-done(((bf16[128,128]{1,0:T(8,128)(2,1)}), bf16[4096,128]{1,0:T(8,128)(2,1)}) %all-gather.12.cloned.1.call-update) | async-done | bytes 1048592 | tf_op jit(solution)/shard_map/all_gather | solution.py:44
  94.2 2.6 convolution_convert_fusion.3
  96.8 1.6 copy.22
  98.5 74.9 %all-gather.16.cloned.1.call-done = bf16[4096,128]{1,0:T(8,128)(2,1)} async-done(((bf16[128,128]{1,0:T(8,128)(2,1)}), bf16[4096,128]{1,0:T(8,128)(2,1)}) %all-gather.16.cloned.1.call-update) | async-done | bytes 1048592 | tf_op jit(solution)/shard_map/all_gather | solution.py:45
  173.4 1.9 convolution_convert_fusion.2
  175.3 0.7 copy.25
  176.0 2.7 stack.2
  178.8 6.9 all-to-all-start
  185.7 0.7 all-gather.20.cloned.1.call-update
  186.4 0.2 reduce-scatter.2.cloned.1.call-start
  186.8 0.1 iota_compare_fusion.1
  186.9 2.8 fusion.16
  189.6 43.5 %all-to-all-done = bf16[32,2,128,1,128]{4,2,1,3,0:T(8,128)(2,1)} async-done(((bf16[32,2,128,1,128]{4,2,1,3,0:T(8,128)(2,1)}), bf16[32,2,128,1,128]{4,2,1,3,0:T(8,128)(2,1)}, u32[]{:S(2)}, u32[]{:S(2)}) %all-to-all-start) | async-done | bytes 2097184 | tf_op jit(solution)/shard_map/all_to_all | solution.py:67
  233.2 3.1 copy.20
  236.3 74.8 %all-gather.8.cloned.1.call-done = bf16[4096,512]{1,0:T(8,128)(2,1)} async-done(((bf16[128,512]{1,0:T(8,128)(2,1)}), bf16[4096,512]{1,0:T(8,128)(2,1)}) %all-gather.8.cloned.1.call-update) | async-done | bytes 4194320 | tf_op jit(solution)/shard_map/all_gather | solution.py:43
  311.1 4.1 convolution_convert_fusion.1
  315.2 1.0 reshape.181
  316.2 9.6 %fusion = (f32[2,4,128]{2,1,0:T(4,128)S(1)}, f32[2,128,4,4096]{3,1,2,0:T(8,128)}) fusion(pred[2,128,4096]{2,1,0:T(8,128)(4,1)} %get-tuple-element.20, bf16[2,4096,128,1]{2,1,3,0:T(8,128)(2,1)} %bitcast.121, bf16[2,128,4,128]{3,2,1,0:T(4,128)(2,1)S(1)} %reshape.181), kind=kOutput, calls=%fused_computation.4 | convolution fusion | flops 1086323712 | bytes 20189184 | tf_op jit(solution)/shard_map/rqkgd,rpkd->rkgqp/dot_general | solution.py:13
  325.9 74.8 %all-gather.14.cloned.1.call-done = bf16[2,4096,1,128]{3,1,0,2:T(8,128)(2,1)} async-done(((bf16[2,128,1,128]{3,1,0,2:T(8,128)(2,1)}), bf16[2,4096,1,128]{3,1,0,2:T(8,128)(2,1)}) %all-gather.14.cloned.1.call-update) | async-done | bytes 2097168 | tf_op jit(solution)/shard_map/all_gather | solution.py:78
  400.7 4.9 fusion.1
  405.6 14.2 %fusion.2 = f32[2,4,128]{2,1,0:T(4,128)S(1)} fusion(f32[2,128,4,4096]{3,1,2,0:T(8,128)} %get-tuple-element.17, f32[2,4,128]{2,1,0:T(4,128)S(1)} %get-tuple-element.15, pred[2,128,4096]{2,1,0:T(8,128)(4,1)S(1)} %copy-done.2), kind=kLoop, calls=%fused_computation.6 | loop fusion | flops 20970496 | bytes 17833984 | tf_op jit(solution)/shard_map/reduce_sum | solution.py:20
  419.8 5.0 fusion.4
  424.8 72.1 %all-gather.10.cloned.1.call-done = bf16[2,4096,1,128]{1,3,0,2:T(8,128)(2,1)} async-done(((bf16[2,128,1,128]{1,3,0,2:T(8,128)(2,1)}), bf16[2,4096,1,128]{1,3,0,2:T(8,128)(2,1)}) %all-gather.10.cloned.1.call-update) | async-done | bytes 2097168 | tf_op jit(solution)/shard_map/all_gather | solution.py:69
  497.0 10.6 %fusion.32 = f32[2,4,128,128]{2,3,1,0:T(8,128)} fusion(bf16[2,4096,1,128]{1,3,0,2:T(8,128)(2,1)} %all-gather.10.cloned.1.call-done, f32[2,128,4,4096]{3,1,2,0:T(8,128)} %get-tuple-element.17, f32[2,4,128]{2,1,0:T(4,128)S(1)} %get-tuple-element.15, pred[2,128,4096]{2,1,0:T(8,128)(4,1)} %get-tuple-element.20, f32[2,4,128]{2,1,0:T(4,128)S(1)} %get-tuple-element.10, ...), kind=kOutput, calls=%fused_computation.30 | convolution fusion | flops 1094975488 | bytes 20459520 | tf_op jit(solution)/shard_map/rkgqp,rpkd->rkgqd/dot_general | solution.py:21
  507.6 87.3 %all-gather.18.cloned.1.call-done = bf16[2,4096,1,128]{1,3,0,2:T(8,128)(2,1)} async-done(((bf16[2,128,1,128]{1,3,0,2:T(8,128)(2,1)}), bf16[2,4096,1,128]{1,3,0,2:T(8,128)(2,1)}) %all-gather.18.cloned.1.call-update) | async-done | bytes 2097168 | tf_op jit(solution)/shard_map/all_gather | solution.py:79
  594.9 9.7 %fusion.42 = bf16[2,4,128,128]{2,3,1,0:T(8,128)(2,1)S(1)} fusion(f32[2,4,128,128]{2,3,1,0:T(8,128)} %fusion.32, bf16[2,4096,1,128]{1,3,0,2:T(8,128)(2,1)} %all-gather.18.cloned.1.call-done, f32[2,4096,128,4]{1,2,3,0:T(8,128)} %copy-done.1, f32[2,4,128]{2,1,0:T(4,128)S(1)} %get-tuple-element.14, pred[2,128,4096]{2,1,0:T(8,128)(4,1)S(1)} %get-tuple-element.21, ...), kind=kOutput, calls=%fused_computation.35 | convolution fusion | flops 1095106560 | bytes 20717568 | tf_op jit(solution)/shard_map/rkgqp,rpkd->rkgqd/dot_general | solution.py:21
  604.7 100.7 %all-gather.20.cloned.1.call-done = bf16[4096,512]{1,0:T(8,128)(2,1)} async-done(((bf16[128,512]{1,0:T(8,128)(2,1)}), bf16[4096,512]{1,0:T(8,128)(2,1)}) %all-gather.20.cloned.1.call-update) | async-done | bytes 4194320 | tf_op jit(solution)/shard_map/all_gather | solution.py:91
  705.4 4.8 convolution_convert_fusion
  710.2 37.5 %reduce-scatter.2.cloned.1.call-done = bf16[2,128,512]{2,1,0:T(8,128)(2,1)} async-done(((bf16[2,128,4096]{2,1,0:T(8,128)(2,1)}), bf16[2,128,512]{2,1,0:T(8,128)(2,1)}) %reduce-scatter.2.cloned.1.call-update) | async-done | bytes 262160 | tf_op jit(solution)/shard_map/reduce_scatter | solution.py:95
  (27 shorter events, 0.5 us)
Async XLA Ops:
  7.2 87.1 %copy-start = (bf16[2,128,4096]{2,1,0:T(8,128)(2,1)S(1)}, bf16[2,128,4096]{2,1,0:T(8,128)(2,1)}, u32[]{:S(2)}) copy-start(bf16[2,128,4096]{2,1,0:T(8,128)(2,1)} %param.9) | copy-start | bytes 6291460
  7.2 179.5 %copy-start.4 = (s32[2,4096]{1,0:T(2,128)S(1)}, s32[2,4096]{1,0:T(2,128)}, u32[]{:S(2)}) copy-start(s32[2,4096]{1,0:T(2,128)} %param.10) | copy-start | bytes 98308
  7.2 179.5 %copy-start.5 = (s32[2]{0:T(128)S(1)}, s32[2]{0:T(128)}, u32[]{:S(2)}) copy-start(s32[2]{0:T(128)} %param.11) | copy-start | bytes 28
  7.2 87.0 %all-gather.12.cloned.1.call-start = ((), (), s32[]{:S(2)}) async-start(), calls=%async_computation.4 | async-start | bytes 1081344 | tf_op jit(solution)/shard_map/all_gather | solution.py:44
  7.9 165.4 %all-gather.16.cloned.1.call-start = ((), (), s32[]{:S(2)}) async-start(), calls=%async_computation.6 | async-start | bytes 1081344 | tf_op jit(solution)/shard_map/all_gather | solution.py:45
  8.7 302.4 %all-gather.8.cloned.1.call-start = ((), (), s32[]{:S(2)}) async-start(), calls=%async_computation.2 | async-start | bytes 4325376 | tf_op jit(solution)/shard_map/all_gather | solution.py:43
  9.4 391.3 %all-gather.14.cloned.1.call-start = ((), (), s32[]{:S(2)}) async-start(), calls=%async_computation.5 | async-start | bytes 2162688 | tf_op jit(solution)/shard_map/all_gather | solution.py:78
  96.8 400.2 %all-gather.10.cloned.1.call-start = ((), (), s32[]{:S(2)}) async-start(), calls=%async_computation.3 | async-start | bytes 2162688 | tf_op jit(solution)/shard_map/all_gather | solution.py:69
  98.4 496.5 %all-gather.18.cloned.1.call-start = ((), (), s32[]{:S(2)}) async-start(), calls=%async_computation.7 | async-start | bytes 2162688 | tf_op jit(solution)/shard_map/all_gather | solution.py:79
  175.3 139.9 %copy-start.3 = (bf16[256,128]{1,0:T(8,128)(2,1)}, bf16[256,128]{1,0:T(8,128)(2,1)S(1)}, u32[]{:S(2)}) copy-start(bf16[256,128]{1,0:T(8,128)(2,1)S(1)} %convolution_convert_fusion.2) | copy-start | bytes 196612
  178.8 54.4 %all-to-all-start = ((bf16[32,2,128,1,128]{4,2,1,3,0:T(8,128)(2,1)}), bf16[32,2,128,1,128]{4,2,1,3,0:T(8,128)(2,1)}, u32[]{:S(2)}, u32[]{:S(2)}) async-start(bf16[32,2,128,1,128]{4,2,1,3,0:T(8,128)(2,1)} %stack.2), calls=%async_computation | async-start | bytes 4194304 | tf_op jit(solution)/shard_map/all_to_all | solution.py:67
  185.7 519.7 %all-gather.20.cloned.1.call-start = ((), (), s32[]{:S(2)}) async-start(), calls=%async_computation.8 | async-start | bytes 4325376 | tf_op jit(solution)/shard_map/all_gather | solution.py:91
  186.4 561.3 %reduce-scatter.2.cloned.1.call-start = ((), (), s32[]{:S(2)}) async-start(), calls=%async_computation.9 | async-start | bytes 2359296 | tf_op jit(solution)/shard_map/reduce_scatter | solution.py:95
  400.7 4.9 copy-start.2
  405.6 14.2 %copy-start.1 = (f32[2,4096,128,4]{1,2,3,0:T(8,128)}, f32[2,4096,128,4]{1,2,3,0:T(8,128)S(1)}, u32[]{:S(2)}) copy-start(f32[2,4096,128,4]{1,2,3,0:T(8,128)S(1)} %get-tuple-element.19) | copy-start | bytes 50331652
Sparse Core Ops, SparseCore 0:
  11.4 82.7 all-gather.11
  97.6 75.6 all-gather.15
  176.9 134.1 all-gather.7
  315.1 85.6 all-gather.13
  403.8 93.1 all-gather.9
  500.0 94.8 all-gather.17
  598.4 106.9 all-gather.19
  710.4 37.3 reduce-scatter.1
